TPU v7x, 32 devices: a whole 2x2x4 slice. The times are simulated.
32 devices in a mesh: row: 4 (over y, x), col: 8 (over z, core).
Axes of the slice: x: 2, y: 2, z: 4, core: 2. Of those that a mesh axis runs over, the one named last changes fastest.
Arguments:
- frames: bfloat16 [4096, 440], P('col'), may hold values from -6 to 6
- center_picks: int32 [8, 8, 64], P('col'), may hold values from 0 to 511, as said below
- send_counts: int32 [8, 8], P(None, 'col'), may hold values from 0 to 64, as said below
- send_offsets: int32 [8, 8], P(None, 'col'), may hold values from 0 to 256, as said below
Outputs:
- factor_panels: float32 [4, 512, 1024], P('row', 'col')
- trailing: float32 [4, 512, 8, 256], P('row', None, 'col')
Inputs may be any that keep to these rules, and one draw needn't show every extreme that they name: `center_picks`: for each owner the entries over all destinations and slots are distinct local frame indices. `send_counts`: for each destination the counts over owners sum to 256; every destination has an owner that fills all 64 slots and one that sends nothing. `send_offsets`: for each destination the owners' segments [offset, offset + count) cover 0 to 255 without intersection, in an order that varies by destination; an owner that sends nothing may start at 256.
All inputs are finite; a program needn't handle non-finite values.
Results may differ from a plain program's by a relative error of at most 0.0003.
Values may be sent and summed in bfloat16 or wider, within the bound.
No kernel may reach another device: no remote copies, remote signals or barrier semaphores. Data moves between devices by JAX's collectives and lax.ppermute only.
A program may use at most 128 MiB of HBM per device.

v0:
```python
import jax
import jax.numpy as jnp
from jax import lax
from jax.sharding import PartitionSpec as P

PANEL = 256
PANELS = 4
CENT_DEV = 256
kernel_scale = 0.6
ridge_shift = 0.1


def spread(value, axis, source):
    kept = jnp.where(lax.axis_index(axis) == source, value, 0).astype(value.dtype)
    return lax.psum(kept, axis)


def gaussian(left_feats, right_feats):
    inner = lax.dot_general(
        left_feats, right_feats, (((1,), (1,)), ((), ())), preferred_element_type=jnp.float32
    )
    left_norm = jnp.sum(jnp.square(left_feats.astype(jnp.float32)), axis=1)
    right_norm = jnp.sum(jnp.square(right_feats.astype(jnp.float32)), axis=1)
    feat_width = left_feats.shape[1]
    return jnp.exp(
        -(kernel_scale / feat_width) * (left_norm[:, None] + right_norm[None, :] - 2.0 * inner)
    )


def outer_minus(column, panel_cols, rows_piece):
    return column - lax.dot_general(
        panel_cols,
        rows_piece,
        (((1,), (1,)), ((), ())),
        precision=lax.Precision.HIGHEST,
        preferred_element_type=jnp.float32,
    )


def make_panel(column, factor, row_tile, panel_step):
    solved = jax.scipy.linalg.solve_triangular(factor, column.T, lower=True).T
    repeated = jnp.tile(factor, (column.shape[0] // factor.shape[0], 1))
    return jnp.where(
        (row_tile > panel_step)[:, None],
        solved,
        jnp.where((row_tile == panel_step)[:, None], repeated, jnp.zeros_like(solved)),
    )


def update_slots(columns, panel_cols, col_rows):
    columns[0] = outer_minus(columns[0], panel_cols, col_rows)
    return columns


def per_device(frames, center_picks, send_counts, send_offsets):
    rows_axis = lax.axis_size("row")
    cols_axis = lax.axis_size("col")
    row_id = lax.axis_index("row")
    col_id = lax.axis_index("col")
    feat_width = frames.shape[1]
    capacity = center_picks.shape[2]
    outgoing = frames[center_picks[0]]
    incoming = lax.all_to_all(outgoing, "col", split_axis=0, concat_axis=0, tiled=True)
    position = jnp.arange(CENT_DEV, dtype=jnp.int32)
    starts = send_offsets[:, 0]
    lengths = send_counts[:, 0]
    inside = (position[:, None] >= starts[None, :]) & (
        position[:, None] < (starts + lengths)[None, :]
    )
    source = jnp.sum(jnp.where(inside, jnp.arange(cols_axis, dtype=jnp.int32)[None, :], 0), axis=1)
    within = position - jnp.sum(jnp.where(inside, starts[None, :], 0), axis=1)
    own_feats = incoming.reshape(cols_axis * capacity, feat_width)[source * capacity + within]
    col_slots = CENT_DEV // PANEL
    row_tiles_dev = col_slots * cols_axis // rows_axis
    rows_dev = row_tiles_dev * PANEL
    tile_range = jnp.arange(row_tiles_dev, dtype=jnp.int32)
    gathered = lax.all_gather(own_feats, "col", axis=0, tiled=True)
    blocks = gathered.reshape(cols_axis, col_slots, PANEL, feat_width)
    my_tiles = row_id + rows_axis * tile_range
    row_feats = blocks[my_tiles % cols_axis, my_tiles // cols_axis].reshape(rows_dev, feat_width)
    local_rows = jnp.arange(rows_dev, dtype=jnp.int32)
    row_tile = row_id + rows_axis * (local_rows // PANEL)
    global_row = row_tile * PANEL + local_rows % PANEL
    local_cols = jnp.arange(CENT_DEV, dtype=jnp.int32)
    global_col = (col_id + cols_axis * (local_cols // PANEL)) * PANEL + local_cols % PANEL
    kernel = gaussian(row_feats, own_feats) + ridge_shift * (
        global_row[:, None] == global_col[None, :]
    ).astype(jnp.float32)
    columns = [kernel]
    panels = []
    for panel_step in range(PANELS):
        slot_now = panel_step // cols_axis
        tile_slot = panel_step // rows_axis
        diag_here = columns[slot_now][tile_slot * PANEL : (tile_slot + 1) * PANEL]
        diag_block = spread(diag_here, "row", panel_step % rows_axis)
        factor = jnp.linalg.cholesky(diag_block)
        panel_here = make_panel(columns[slot_now], factor, row_tile, panel_step)
        panel_cols = spread(panel_here, "col", panel_step % cols_axis)
        here_rows = lax.dynamic_slice_in_dim(
            panel_cols, (col_id + 0) // rows_axis * PANEL, PANEL, 0
        )
        col_rows = spread(here_rows, "row", col_id % rows_axis)
        panels.append(panel_cols)
        columns = update_slots(columns, panel_cols, col_rows)
    trailing = columns[0].reshape(1, rows_dev, 1, CENT_DEV)
    every_panel = jnp.concatenate(panels, axis=1)
    share_rows = rows_dev // cols_axis
    panel_share = lax.dynamic_slice_in_dim(every_panel, col_id * share_rows, share_rows, 0).reshape(
        1, share_rows, PANELS * PANEL
    )
    return (panel_share, trailing)


def solution(mesh):
    in_specs = (P("col", None), P("col", None, None), P(None, "col"), P(None, "col"))
    out_specs = (P("row", "col", None), P("row", None, "col", None))
    return jax.shard_map(
        per_device, mesh=mesh, in_specs=in_specs, out_specs=out_specs, check_vma=False
    )
```

profile of v0, /device:TPU:0, one launch (start us, length us, event | category | flops | bytes accessed | tf_op | source)
XLA Modules:
  0.0 926.6 jit_solution(15417714206202597751)
XLA Ops:
  7.2 1.2 copy.43
  9.2 2.6 gather_fusion
  11.8 6.3 all-to-all-start
  18.3 15.2 %all-to-all-done = bf16[8,64,440]{2,1,0:T(8,128)(2,1)S(1)} async-done(((bf16[8,64,440]{2,1,0:T(8,128)(2,1)}), bf16[8,64,440]{2,1,0:T(8,128)(2,1)S(1)}, u32[]{:S(2)}, u32[]{:S(2)}) %all-to-all-start) | async-done | bytes 450592 | tf_op jit(solution)/shard_map/all_to_all | solution.py:63
  33.5 1.9 gather_fusion.1
  35.5 1.1 multiply_reduce_fusion.1
  36.6 27.0 %all-gather.3.cloned.1.call-done = bf16[2048,440]{1,0:T(8,128)(2,1)} async-done(((bf16[256,440]{1,0:T(8,128)(2,1)}), bf16[2048,440]{1,0:T(8,128)(2,1)}) %all-gather.3.cloned.1.call-update) | async-done | bytes 1802256 | tf_op jit(solution)/shard_map/all_gather | solution.py:77
  63.5 2.2 gather_fusion.2
  67.6 42.3 %all-reduce.14.cloned.1.call-done = f32[256,256]{0,1:T(8,128)} async-done(((f32[256,256]{0,1:T(8,128)}), f32[256,256]{0,1:T(8,128)}) %all-reduce.14.cloned.1.call-update) | async-done | bytes 262160 | tf_op jit(solution)/shard_map/psum | solution.py:15
  109.9 1.1 copy.45
  111.0 1.0 fusion.26
  112.0 11.7 %cholesky.214 = f32[128,128]{1,0:T(8,128)S(1)} custom-call(f32[128,128]{1,0:T(8,128)S(1)} %cholesky.346), custom_call_target="Cholesky" | custom-call | tf_op jit(solution)/shard_map/jit(cholesky)/cholesky | solution.py:96
  123.7 9.8 %custom-call.19 = f32[1,128,128]{1,2,0:T(8,128)S(1)} custom-call(f32[1,128,128]{2,1,0:T(8,128)S(1)} %get-tuple-element.105), custom_call_target="InvertDiagBlocksLowerTriangular" | custom-call | tf_op jit(solution)/shard_map/jit(cholesky)/cholesky | solution.py:96
  134.0 11.7 %cholesky.231 = f32[128,128]{1,0:T(8,128)S(1)} custom-call(f32[128,128]{1,0:T(8,128)S(1)} %convolution_subtract_fusion.8), custom_call_target="Cholesky" | custom-call | tf_op jit(solution)/shard_map/jit(cholesky)/cholesky | solution.py:96
  148.0 4.6 while.8
  149.1 1.4 bitcast_dynamic-update-slice_fusion.8
  151.1 1.4 bitcast_dynamic-update-slice_fusion.8
  152.6 19.7 %custom-call.20 = f32[2,128,128]{1,2,0:T(8,128)S(1)} custom-call(f32[2,128,128]{2,1,0:T(8,128)S(1)} %get-tuple-element.30), custom_call_target="InvertDiagBlocksLowerTriangular" | custom-call | tf_op jit(solution)/shard_map/jit(_solve_triangular)/triangular_solve | solution.py:41
  174.8 56.2 %all-reduce.16.cloned.1.call-done = f32[512,256]{0,1:T(8,128)} async-done(((f32[512,256]{0,1:T(8,128)}), f32[512,256]{0,1:T(8,128)}) %all-reduce.16.cloned.1.call-update) | async-done | bytes 524304 | tf_op jit(solution)/shard_map/psum | solution.py:15
  231.1 1.7 dynamic-slice_select_fusion.3
  232.8 43.5 %all-reduce.18.cloned.1.call-done = f32[256,256]{0,1:T(8,128)} async-done(((f32[256,256]{0,1:T(8,128)}), f32[256,256]{0,1:T(8,128)}) %all-reduce.18.cloned.1.call-update) | async-done | bytes 262160 | tf_op jit(solution)/shard_map/psum | solution.py:15
  276.4 1.8 bitcast_subtract_fusion.2
  279.2 43.7 %all-reduce.20.cloned.1.call-done = f32[256,256]{0,1:T(8,128)} async-done(((f32[256,256]{0,1:T(8,128)}), f32[256,256]{0,1:T(8,128)}) %all-reduce.20.cloned.1.call-update) | async-done | bytes 262160 | tf_op jit(solution)/shard_map/psum | solution.py:15
  322.9 1.1 copy.48
  324.0 1.0 fusion.25
  325.0 11.7 %cholesky.248 = f32[128,128]{1,0:T(8,128)S(1)} custom-call(f32[128,128]{1,0:T(8,128)S(1)} %cholesky.349), custom_call_target="Cholesky" | custom-call | tf_op jit(solution)/shard_map/jit(cholesky)/cholesky | solution.py:96
  336.8 9.8 %custom-call.21 = f32[1,128,128]{1,2,0:T(8,128)S(1)} custom-call(f32[1,128,128]{2,1,0:T(8,128)S(1)} %get-tuple-element.101), custom_call_target="InvertDiagBlocksLowerTriangular" | custom-call | tf_op jit(solution)/shard_map/jit(cholesky)/cholesky | solution.py:96
  347.1 11.7 %cholesky.265 = f32[128,128]{1,0:T(8,128)S(1)} custom-call(f32[128,128]{1,0:T(8,128)S(1)} %convolution_subtract_fusion.7), custom_call_target="Cholesky" | custom-call | tf_op jit(solution)/shard_map/jit(cholesky)/cholesky | solution.py:96
  361.6 4.3 while.9
  362.4 1.4 bitcast_dynamic-update-slice_fusion.9
  364.4 1.4 bitcast_dynamic-update-slice_fusion.9
  365.9 19.7 %custom-call.22 = f32[2,128,128]{1,2,0:T(8,128)S(1)} custom-call(f32[2,128,128]{2,1,0:T(8,128)S(1)} %get-tuple-element.31), custom_call_target="InvertDiagBlocksLowerTriangular" | custom-call | tf_op jit(solution)/shard_map/jit(_solve_triangular)/triangular_solve | solution.py:41
  388.1 56.3 %all-reduce.22.cloned.1.call-done = f32[512,256]{0,1:T(8,128)} async-done(((f32[512,256]{0,1:T(8,128)}), f32[512,256]{0,1:T(8,128)}) %all-reduce.22.cloned.1.call-update) | async-done | bytes 524304 | tf_op jit(solution)/shard_map/psum | solution.py:15
  444.4 1.7 dynamic-slice_select_fusion.2
  446.2 43.9 %all-reduce.24.cloned.1.call-done = f32[256,256]{0,1:T(8,128)} async-done(((f32[256,256]{0,1:T(8,128)}), f32[256,256]{0,1:T(8,128)}) %all-reduce.24.cloned.1.call-update) | async-done | bytes 262160 | tf_op jit(solution)/shard_map/psum | solution.py:15
  490.1 1.8 bitcast_subtract_fusion.1
  492.8 43.8 %all-reduce.26.cloned.1.call-done = f32[256,256]{0,1:T(8,128)} async-done(((f32[256,256]{0,1:T(8,128)}), f32[256,256]{0,1:T(8,128)}) %all-reduce.26.cloned.1.call-update) | async-done | bytes 262160 | tf_op jit(solution)/shard_map/psum | solution.py:15
  536.6 1.1 copy.52
  538.6 11.7 %cholesky.282 = f32[128,128]{1,0:T(8,128)S(1)} custom-call(f32[128,128]{1,0:T(8,128)S(1)} %cholesky.352), custom_call_target="Cholesky" | custom-call | tf_op jit(solution)/shard_map/jit(cholesky)/cholesky | solution.py:96
  550.4 9.8 %custom-call.23 = f32[1,128,128]{1,2,0:T(8,128)S(1)} custom-call(f32[1,128,128]{2,1,0:T(8,128)S(1)} %get-tuple-element.97), custom_call_target="InvertDiagBlocksLowerTriangular" | custom-call | tf_op jit(solution)/shard_map/jit(cholesky)/cholesky | solution.py:96
  560.7 11.7 %cholesky.299 = f32[128,128]{1,0:T(8,128)S(1)} custom-call(f32[128,128]{1,0:T(8,128)S(1)} %convolution_subtract_fusion.6), custom_call_target="Cholesky" | custom-call | tf_op jit(solution)/shard_map/jit(cholesky)/cholesky | solution.py:96
  575.2 4.3 while.10
  576.0 1.4 bitcast_dynamic-update-slice_fusion.10
  578.1 1.4 bitcast_dynamic-update-slice_fusion.10
  579.5 19.7 %custom-call.24 = f32[2,128,128]{1,2,0:T(8,128)S(1)} custom-call(f32[2,128,128]{2,1,0:T(8,128)S(1)} %get-tuple-element.32), custom_call_target="InvertDiagBlocksLowerTriangular" | custom-call | tf_op jit(solution)/shard_map/jit(_solve_triangular)/triangular_solve | solution.py:41
  601.8 56.3 %all-reduce.28.cloned.1.call-done = f32[512,256]{0,1:T(8,128)} async-done(((f32[512,256]{0,1:T(8,128)}), f32[512,256]{0,1:T(8,128)}) %all-reduce.28.cloned.1.call-update) | async-done | bytes 524304 | tf_op jit(solution)/shard_map/psum | solution.py:15
  658.1 1.7 dynamic-slice_select_fusion.1
  659.8 43.5 %all-reduce.30.cloned.1.call-done = f32[256,256]{0,1:T(8,128)} async-done(((f32[256,256]{0,1:T(8,128)}), f32[256,256]{0,1:T(8,128)}) %all-reduce.30.cloned.1.call-update) | async-done | bytes 262160 | tf_op jit(solution)/shard_map/psum | solution.py:15
  703.3 1.8 bitcast_subtract_fusion
  706.0 44.0 %all-reduce.32.cloned.1.call-done = f32[256,256]{0,1:T(8,128)} async-done(((f32[256,256]{0,1:T(8,128)}), f32[256,256]{0,1:T(8,128)}) %all-reduce.32.cloned.1.call-update) | async-done | bytes 262160 | tf_op jit(solution)/shard_map/psum | solution.py:15
  750.1 1.1 copy.56
  752.1 11.7 %cholesky.316 = f32[128,128]{1,0:T(8,128)S(1)} custom-call(f32[128,128]{1,0:T(8,128)S(1)} %cholesky.355), custom_call_target="Cholesky" | custom-call | tf_op jit(solution)/shard_map/jit(cholesky)/cholesky | solution.py:96
  763.9 9.8 %custom-call.25 = f32[1,128,128]{1,2,0:T(8,128)S(1)} custom-call(f32[1,128,128]{2,1,0:T(8,128)S(1)} %get-tuple-element.93), custom_call_target="InvertDiagBlocksLowerTriangular" | custom-call | tf_op jit(solution)/shard_map/jit(cholesky)/cholesky | solution.py:96
  774.2 11.7 %cholesky.333 = f32[128,128]{1,0:T(8,128)S(1)} custom-call(f32[128,128]{1,0:T(8,128)S(1)} %convolution_subtract_fusion.5), custom_call_target="Cholesky" | custom-call | tf_op jit(solution)/shard_map/jit(cholesky)/cholesky | solution.py:96
  788.6 4.2 while.11
  789.5 1.3 bitcast_dynamic-update-slice_fusion.11
  791.4 1.3 bitcast_dynamic-update-slice_fusion.11
  792.8 19.7 %custom-call.26 = f32[2,128,128]{1,2,0:T(8,128)S(1)} custom-call(f32[2,128,128]{2,1,0:T(8,128)S(1)} %get-tuple-element.33), custom_call_target="InvertDiagBlocksLowerTriangular" | custom-call | tf_op jit(solution)/shard_map/jit(_solve_triangular)/triangular_solve | solution.py:41
  815.1 56.3 %all-reduce.34.cloned.1.call-done = f32[512,256]{0,1:T(8,128)} async-done(((f32[512,256]{0,1:T(8,128)}), f32[512,256]{0,1:T(8,128)}) %all-reduce.34.cloned.1.call-update) | async-done | bytes 524304 | tf_op jit(solution)/shard_map/psum | solution.py:15
  871.3 1.7 dynamic-slice_select_fusion
  873.1 1.1 fusion.3
  875.1 41.9 %all-reduce.36.cloned.1.call-done = f32[256,256]{0,1:T(8,128)} async-done(((f32[256,256]{0,1:T(8,128)}), f32[256,256]{0,1:T(8,128)}) %all-reduce.36.cloned.1.call-update) | async-done | bytes 262160 | tf_op jit(solution)/shard_map/psum | solution.py:15
  917.0 1.6 fusion
  918.6 1.0 copy.61
  (154 shorter events, 30.8 us)
Async XLA Ops:
  9.2 9.0 copy-start.5
  9.2 9.0 copy-start.6
  11.8 21.7 %all-to-all-start = ((bf16[8,64,440]{2,1,0:T(8,128)(2,1)}), bf16[8,64,440]{2,1,0:T(8,128)(2,1)S(1)}, u32[]{:S(2)}, u32[]{:S(2)}) async-start(bf16[8,64,440]{2,1,0:T(8,128)(2,1)} %bitcast.1), calls=%async_computation | async-start | bytes 1048576 | tf_op jit(solution)/shard_map/all_to_all | solution.py:63
  18.1 45.4 %all-gather.3.cloned.1.call-start = ((), (), s32[]{:S(2)}) async-start(), calls=%async_computation.13 | async-start | bytes 2359296 | tf_op jit(solution)/shard_map/all_gather | solution.py:77
  35.3 30.6 %copy-start.4 = (bf16[256,440]{1,0:T(8,128)(2,1)S(1)}, bf16[256,440]{1,0:T(8,128)(2,1)}, u32[]{:S(2)}) copy-start(bf16[256,440]{1,0:T(8,128)(2,1)} %gather_fusion.1) | copy-start | bytes 675844
  35.4 74.5 %all-reduce.14.cloned.1.call-start = ((), (), s32[]{:S(2)}) async-start(), calls=%async_computation.1 | async-start | bytes 524288 | tf_op jit(solution)/shard_map/psum | solution.py:15
  67.3 163.8 %all-reduce.16.cloned.1.call-start = ((), (), s32[]{:S(2)}) async-start(), calls=%async_computation.2 | async-start | bytes 1048576 | tf_op jit(solution)/shard_map/psum | solution.py:15
  174.8 101.6 %all-reduce.18.cloned.1.call-start = ((), (), s32[]{:S(2)}) async-start(), calls=%async_computation.3 | async-start | bytes 524288 | tf_op jit(solution)/shard_map/psum | solution.py:15
  232.8 90.2 %all-reduce.20.cloned.1.call-start = ((), (), s32[]{:S(2)}) async-start(), calls=%async_computation.4 | async-start | bytes 524288 | tf_op jit(solution)/shard_map/psum | solution.py:15
  279.1 165.3 %all-reduce.22.cloned.1.call-start = ((), (), s32[]{:S(2)}) async-start(), calls=%async_computation.5 | async-start | bytes 1048576 | tf_op jit(solution)/shard_map/psum | solution.py:15
  388.1 102.0 %all-reduce.24.cloned.1.call-start = ((), (), s32[]{:S(2)}) async-start(), calls=%async_computation.6 | async-start | bytes 524288 | tf_op jit(solution)/shard_map/psum | solution.py:15
  446.1 90.5 %all-reduce.26.cloned.1.call-start = ((), (), s32[]{:S(2)}) async-start(), calls=%async_computation.7 | async-start | bytes 524288 | tf_op jit(solution)/shard_map/psum | solution.py:15
  492.7 165.4 %all-reduce.28.cloned.1.call-start = ((), (), s32[]{:S(2)}) async-start(), calls=%async_computation.8 | async-start | bytes 1048576 | tf_op jit(solution)/shard_map/psum | solution.py:15
  601.7 101.6 %all-reduce.30.cloned.1.call-start = ((), (), s32[]{:S(2)}) async-start(), calls=%async_computation.9 | async-start | bytes 524288 | tf_op jit(solution)/shard_map/psum | solution.py:15
  659.8 90.3 %all-reduce.32.cloned.1.call-start = ((), (), s32[]{:S(2)}) async-start(), calls=%async_computation.10 | async-start | bytes 524288 | tf_op jit(solution)/shard_map/psum | solution.py:15
  706.0 165.4 %all-reduce.34.cloned.1.call-start = ((), (), s32[]{:S(2)}) async-start(), calls=%async_computation.11 | async-start | bytes 1048576 | tf_op jit(solution)/shard_map/psum | solution.py:15
  814.0 59.1 %copy-start.1 = (f32[512,256]{0,1:T(8,128)S(1)}, f32[512,256]{0,1:T(8,128)}, u32[]{:S(2)}) copy-start(f32[512,256]{0,1:T(8,128)} %all-reduce.16.cloned.1.call-done) | copy-start | bytes 1572868
  814.0 59.1 %copy-start.2 = (f32[512,256]{0,1:T(8,128)S(1)}, f32[512,256]{0,1:T(8,128)}, u32[]{:S(2)}) copy-start(f32[512,256]{0,1:T(8,128)} %all-reduce.22.cloned.1.call-done) | copy-start | bytes 1572868
  814.0 59.1 %copy-start.3 = (f32[512,256]{0,1:T(8,128)S(1)}, f32[512,256]{0,1:T(8,128)}, u32[]{:S(2)}) copy-start(f32[512,256]{0,1:T(8,128)} %all-reduce.28.cloned.1.call-done) | copy-start | bytes 1572868
  815.0 102.0 %all-reduce.36.cloned.1.call-start = ((), (), s32[]{:S(2)}) async-start(), calls=%async_computation.12 | async-start | bytes 524288 | tf_op jit(solution)/shard_map/psum | solution.py:15
  871.3 45.7 %copy-start = (f32[512,256]{0,1:T(8,128)S(1)}, f32[512,256]{0,1:T(8,128)}, u32[]{:S(2)}) copy-start(f32[512,256]{0,1:T(8,128)} %all-reduce.34.cloned.1.call-done) | copy-start | bytes 1572868
Sparse Core Ops, SparseCore 0:
  35.5 27.9 all-gather.2
  67.4 42.4 all-reduce.13
  174.9 56.1 all-reduce.15
  234.4 41.8 all-reduce.17
  280.0 42.9 all-reduce.19
  388.2 56.1 all-reduce.21
  448.2 41.8 all-reduce.23
  493.6 42.9 all-reduce.25
  601.9 56.1 all-reduce.27
  661.4 41.9 all-reduce.29
  707.1 42.9 all-reduce.31
  815.1 56.1 all-reduce.33
  875.1 41.8 all-reduce.35
where the time goes:
time: 930 us; the launch traced here: 927 us
  waiting for transfers between devices  614 us (66%)
  other arithmetic  238 us (26%)
  local copies, waits for them, and re-layouts  31.9 us (3%)
  between operations  20.4 us (2%)
  matrix products  14 us (2%)
    psum x12, waiting for transfers between devices, spread(): return lax.psum(kept, axis)  572 us
    another operation x27, other arithmetic, per_device(): factor = jnp.linalg.cholesky(diag_block)  138 us
    another operation x9, other arithmetic, make_panel(): solved = jax.scipy.linalg.solve_triangular(factor, column.T, lower=True).T  78.8 us
    all_gather x1, waiting for transfers between devices, per_device(): gathered = lax.all_gather(own_feats, 'col', axis=0, tiled=True)  27 us
  transfers between devices with their start and end apart: 14, of which 14 were waited for; matrix products, arithmetic and copies ran while one was open for 0% of the time, Pallas kernels for 0%

commit v1 on v0

--- a/solution.py
+++ b/solution.py
@@ -1,3 +1,4 @@
+import functools
 import jax
 import jax.numpy as jnp
 from jax import lax
@@ -8,6 +9,24 @@
 CENT_DEV = 256
 kernel_scale = 0.6
 ridge_shift = 0.1
+
+
+def _store_regions(block_here, dim_no):
+    local_now = lax.axis_size("col")
+    e_next = lax.axis_index("col")
+    row_out, block_now = (local_now, e_next)
+    new, seen_now = (block_here, 1)
+    while seen_now < row_out:
+        known = tuple(((to_i, to_i ^ seen_now) for to_i in range(row_out)))
+        frame_out = lax.ppermute(new, "col", known)
+        passed = jnp.concatenate([new, frame_out], dim_no)
+        oldest = jnp.concatenate([frame_out, new], dim_no)
+        new = jnp.where(block_now & seen_now == 0, passed, oldest)
+        seen_now = 2 * seen_now
+    return new
+
+
+quarters_choose = functools.partial(_store_regions, dim_no=0)
 
 
 def spread(value, axis, source):
@@ -74,7 +93,7 @@
     row_tiles_dev = col_slots * cols_axis // rows_axis
     rows_dev = row_tiles_dev * PANEL
     tile_range = jnp.arange(row_tiles_dev, dtype=jnp.int32)
-    gathered = lax.all_gather(own_feats, "col", axis=0, tiled=True)
+    gathered = quarters_choose(own_feats)
     blocks = gathered.reshape(cols_axis, col_slots, PANEL, feat_width)
     my_tiles = row_id + rows_axis * tile_range
     row_feats = blocks[my_tiles % cols_axis, my_tiles // cols_axis].reshape(rows_dev, feat_width)

time: 930 us -> 964 us (1.037)
  waiting for transfers between devices: 614 us -> 643 us
    ppermute x0 -> x3, waiting for transfers between devices: none -> 56.6 us  [_store_regions(): frame_out = lax.ppermute(new, 'col', known)]
    all_gather x1 -> x0, waiting for transfers between devices: 27 us -> none  [per_device(): gathered = lax.all_gather(own_feats, 'col', axis=0, tiled=True)]
  transfers between devices with their start and end apart: 14 -> 16, of which waited for: 14 -> 16; matrix products, arithmetic and copies ran while one was open for 0% -> 0% of each run, Pallas kernels for 0% -> 0%
where the time goes in v1:
time: 964 us; the launch traced here: 959 us
  waiting for transfers between devices  643 us (67%)
  other arithmetic  240 us (25%)
  local copies, waits for them, and re-layouts  32.2 us (3%)
  between operations  20.8 us (2%)
  matrix products  15.1 us (2%)
    psum x12, waiting for transfers between devices, spread(): return lax.psum(kept, axis)  571 us
    another operation x27, other arithmetic, per_device(): factor = jnp.linalg.cholesky(diag_block)  138 us
    another operation x9, other arithmetic, make_panel(): solved = jax.scipy.linalg.solve_triangular(factor, column.T, lower=True).T  78.8 us
    ppermute x3, waiting for transfers between devices, _store_regions(): frame_out = lax.ppermute(new, 'col', known)  56.6 us
  transfers between devices with their start and end apart: 16, of which 16 were waited for; matrix products, arithmetic and copies ran while one was open for 0% of the time, Pallas kernels for 0%

profile of v1, /device:TPU:0, one launch (start us, length us, event | category | flops | bytes accessed | tf_op | source)
XLA Modules:
  0.0 959.2 jit_solution(3199982636884245283)
XLA Ops:
  7.2 1.2 copy.65
  9.2 2.6 gather_fusion
  11.8 6.3 all-to-all-start
  18.3 15.2 %all-to-all-done = bf16[8,64,440]{2,1,0:T(8,128)(2,1)S(1)} async-done(((bf16[8,64,440]{2,1,0:T(8,128)(2,1)}), bf16[8,64,440]{2,1,0:T(8,128)(2,1)S(1)}, u32[]{:S(2)}, u32[]{:S(2)}) %all-to-all-start) | async-done | bytes 450592 | tf_op jit(solution)/shard_map/all_to_all | solution.py:82
  33.5 1.2 gather_fusion.1
  34.7 1.5 collective-permute-done
  36.5 13.9 %collective-permute-done.1 = bf16[512,440]{1,0:T(8,128)(2,1)S(1)} collective-permute-done((bf16[512,440]{1,0:T(8,128)(2,1)S(1)}, bf16[512,440]{1,0:T(8,128)(2,1)S(1)}, u32[]{:S(2)}, u32[]{:S(2)}) %collective-permute-start.1) | collective-permute-done | bytes 450592 | tf_op jit(solution)/shard_map/ppermute | solution.py:21
  51.7 41.2 %collective-permute-done.2 = bf16[1024,440]{0,1:T(8,128)(2,1)S(1)} collective-permute-done((bf16[1024,440]{0,1:T(8,128)(2,1)S(1)}, bf16[1024,440]{0,1:T(8,128)(2,1)S(1)}, u32[]{:S(2)}, u32[]{:S(2)}) %collective-permute-start.2) | collective-permute-done | bytes 901152 | tf_op jit(solution)/shard_map/ppermute | solution.py:21
  93.4 2.0 maximum_select_fusion
  95.4 2.2 gather_fusion.2
  99.5 41.7 %all-reduce.14.cloned.1.call-done = f32[256,256]{0,1:T(8,128)} async-done(((f32[256,256]{0,1:T(8,128)}), f32[256,256]{0,1:T(8,128)}) %all-reduce.14.cloned.1.call-update) | async-done | bytes 262160 | tf_op jit(solution)/shard_map/psum | solution.py:34
  141.2 1.1 copy.70
  143.2 11.7 %cholesky.214 = f32[128,128]{1,0:T(8,128)S(1)} custom-call(f32[128,128]{1,0:T(8,128)S(1)} %cholesky.346), custom_call_target="Cholesky" | custom-call | tf_op jit(solution)/shard_map/jit(cholesky)/cholesky | solution.py:115
  155.0 9.8 %custom-call.19 = f32[1,128,128]{1,2,0:T(8,128)S(1)} custom-call(f32[1,128,128]{2,1,0:T(8,128)S(1)} %get-tuple-element.107), custom_call_target="InvertDiagBlocksLowerTriangular" | custom-call | tf_op jit(solution)/shard_map/jit(cholesky)/cholesky | solution.py:115
  165.3 11.7 %cholesky.231 = f32[128,128]{1,0:T(8,128)S(1)} custom-call(f32[128,128]{1,0:T(8,128)S(1)} %convolution_subtract_fusion.8), custom_call_target="Cholesky" | custom-call | tf_op jit(solution)/shard_map/jit(cholesky)/cholesky | solution.py:115
  179.6 4.6 while.8
  180.7 1.4 bitcast_dynamic-update-slice_fusion.8
  182.8 1.4 bitcast_dynamic-update-slice_fusion.8
  184.2 19.7 %custom-call.20 = f32[2,128,128]{1,2,0:T(8,128)S(1)} custom-call(f32[2,128,128]{2,1,0:T(8,128)S(1)} %get-tuple-element.30), custom_call_target="InvertDiagBlocksLowerTriangular" | custom-call | tf_op jit(solution)/shard_map/jit(_solve_triangular)/triangular_solve | solution.py:60
  206.1 56.2 %all-reduce.16.cloned.1.call-done = f32[512,256]{0,1:T(8,128)} async-done(((f32[512,256]{0,1:T(8,128)}), f32[512,256]{0,1:T(8,128)}) %all-reduce.16.cloned.1.call-update) | async-done | bytes 524304 | tf_op jit(solution)/shard_map/psum | solution.py:34
  262.4 1.7 dynamic-slice_select_fusion.3
  264.1 43.7 %all-reduce.18.cloned.1.call-done = f32[256,256]{0,1:T(8,128)} async-done(((f32[256,256]{0,1:T(8,128)}), f32[256,256]{0,1:T(8,128)}) %all-reduce.18.cloned.1.call-update) | async-done | bytes 262160 | tf_op jit(solution)/shard_map/psum | solution.py:34
  307.8 1.8 bitcast_subtract_fusion.2
  310.6 43.7 %all-reduce.20.cloned.1.call-done = f32[256,256]{0,1:T(8,128)} async-done(((f32[256,256]{0,1:T(8,128)}), f32[256,256]{0,1:T(8,128)}) %all-reduce.20.cloned.1.call-update) | async-done | bytes 262160 | tf_op jit(solution)/shard_map/psum | solution.py:34
  354.4 1.1 copy.73
  356.5 11.7 %cholesky.248 = f32[128,128]{1,0:T(8,128)S(1)} custom-call(f32[128,128]{1,0:T(8,128)S(1)} %cholesky.349), custom_call_target="Cholesky" | custom-call | tf_op jit(solution)/shard_map/jit(cholesky)/cholesky | solution.py:115
  368.2 9.8 %custom-call.21 = f32[1,128,128]{1,2,0:T(8,128)S(1)} custom-call(f32[1,128,128]{2,1,0:T(8,128)S(1)} %get-tuple-element.103), custom_call_target="InvertDiagBlocksLowerTriangular" | custom-call | tf_op jit(solution)/shard_map/jit(cholesky)/cholesky | solution.py:115
  378.5 11.7 %cholesky.265 = f32[128,128]{1,0:T(8,128)S(1)} custom-call(f32[128,128]{1,0:T(8,128)S(1)} %convolution_subtract_fusion.7), custom_call_target="Cholesky" | custom-call | tf_op jit(solution)/shard_map/jit(cholesky)/cholesky | solution.py:115
  393.4 4.3 while.9
  394.2 1.4 bitcast_dynamic-update-slice_fusion.9
  396.3 1.4 bitcast_dynamic-update-slice_fusion.9
  397.7 19.7 %custom-call.22 = f32[2,128,128]{1,2,0:T(8,128)S(1)} custom-call(f32[2,128,128]{2,1,0:T(8,128)S(1)} %get-tuple-element.31), custom_call_target="InvertDiagBlocksLowerTriangular" | custom-call | tf_op jit(solution)/shard_map/jit(_solve_triangular)/triangular_solve | solution.py:60
  419.6 56.3 %all-reduce.22.cloned.1.call-done = f32[512,256]{0,1:T(8,128)} async-done(((f32[512,256]{0,1:T(8,128)}), f32[512,256]{0,1:T(8,128)}) %all-reduce.22.cloned.1.call-update) | async-done | bytes 524304 | tf_op jit(solution)/shard_map/psum | solution.py:34
  475.9 1.7 dynamic-slice_select_fusion.2
  477.6 43.8 %all-reduce.24.cloned.1.call-done = f32[256,256]{0,1:T(8,128)} async-done(((f32[256,256]{0,1:T(8,128)}), f32[256,256]{0,1:T(8,128)}) %all-reduce.24.cloned.1.call-update) | async-done | bytes 262160 | tf_op jit(solution)/shard_map/psum | solution.py:34
  521.4 1.8 bitcast_subtract_fusion.1
  524.1 43.8 %all-reduce.26.cloned.1.call-done = f32[256,256]{0,1:T(8,128)} async-done(((f32[256,256]{0,1:T(8,128)}), f32[256,256]{0,1:T(8,128)}) %all-reduce.26.cloned.1.call-update) | async-done | bytes 262160 | tf_op jit(solution)/shard_map/psum | solution.py:34
  567.9 1.1 copy.77
  570.0 11.7 %cholesky.282 = f32[128,128]{1,0:T(8,128)S(1)} custom-call(f32[128,128]{1,0:T(8,128)S(1)} %cholesky.352), custom_call_target="Cholesky" | custom-call | tf_op jit(solution)/shard_map/jit(cholesky)/cholesky | solution.py:115
  581.8 9.8 %custom-call.23 = f32[1,128,128]{1,2,0:T(8,128)S(1)} custom-call(f32[1,128,128]{2,1,0:T(8,128)S(1)} %get-tuple-element.99), custom_call_target="InvertDiagBlocksLowerTriangular" | custom-call | tf_op jit(solution)/shard_map/jit(cholesky)/cholesky | solution.py:115
  592.0 11.7 %cholesky.299 = f32[128,128]{1,0:T(8,128)S(1)} custom-call(f32[128,128]{1,0:T(8,128)S(1)} %convolution_subtract_fusion.6), custom_call_target="Cholesky" | custom-call | tf_op jit(solution)/shard_map/jit(cholesky)/cholesky | solution.py:115
  606.9 4.3 while.10
  607.8 1.4 bitcast_dynamic-update-slice_fusion.10
  609.8 1.4 bitcast_dynamic-update-slice_fusion.10
  611.3 19.7 %custom-call.24 = f32[2,128,128]{1,2,0:T(8,128)S(1)} custom-call(f32[2,128,128]{2,1,0:T(8,128)S(1)} %get-tuple-element.32), custom_call_target="InvertDiagBlocksLowerTriangular" | custom-call | tf_op jit(solution)/shard_map/jit(_solve_triangular)/triangular_solve | solution.py:60
  633.1 56.3 %all-reduce.28.cloned.1.call-done = f32[512,256]{0,1:T(8,128)} async-done(((f32[512,256]{0,1:T(8,128)}), f32[512,256]{0,1:T(8,128)}) %all-reduce.28.cloned.1.call-update) | async-done | bytes 524304 | tf_op jit(solution)/shard_map/psum | solution.py:34
  689.4 1.7 dynamic-slice_select_fusion.1
  691.1 43.7 %all-reduce.30.cloned.1.call-done = f32[256,256]{0,1:T(8,128)} async-done(((f32[256,256]{0,1:T(8,128)}), f32[256,256]{0,1:T(8,128)}) %all-reduce.30.cloned.1.call-update) | async-done | bytes 262160 | tf_op jit(solution)/shard_map/psum | solution.py:34
  734.8 1.8 bitcast_subtract_fusion
  737.6 43.8 %all-reduce.32.cloned.1.call-done = f32[256,256]{0,1:T(8,128)} async-done(((f32[256,256]{0,1:T(8,128)}), f32[256,256]{0,1:T(8,128)}) %all-reduce.32.cloned.1.call-update) | async-done | bytes 262160 | tf_op jit(solution)/shard_map/psum | solution.py:34
  781.4 1.1 copy.81
  783.5 11.7 %cholesky.316 = f32[128,128]{1,0:T(8,128)S(1)} custom-call(f32[128,128]{1,0:T(8,128)S(1)} %cholesky.355), custom_call_target="Cholesky" | custom-call | tf_op jit(solution)/shard_map/jit(cholesky)/cholesky | solution.py:115
  795.3 9.8 %custom-call.25 = f32[1,128,128]{1,2,0:T(8,128)S(1)} custom-call(f32[1,128,128]{2,1,0:T(8,128)S(1)} %get-tuple-element.95), custom_call_target="InvertDiagBlocksLowerTriangular" | custom-call | tf_op jit(solution)/shard_map/jit(cholesky)/cholesky | solution.py:115
  805.6 11.7 %cholesky.333 = f32[128,128]{1,0:T(8,128)S(1)} custom-call(f32[128,128]{1,0:T(8,128)S(1)} %convolution_subtract_fusion.5), custom_call_target="Cholesky" | custom-call | tf_op jit(solution)/shard_map/jit(cholesky)/cholesky | solution.py:115
  820.3 4.2 while.11
  821.2 1.3 bitcast_dynamic-update-slice_fusion.11
  823.1 1.3 bitcast_dynamic-update-slice_fusion.11
  824.5 19.7 %custom-call.26 = f32[2,128,128]{1,2,0:T(8,128)S(1)} custom-call(f32[2,128,128]{2,1,0:T(8,128)S(1)} %get-tuple-element.33), custom_call_target="InvertDiagBlocksLowerTriangular" | custom-call | tf_op jit(solution)/shard_map/jit(_solve_triangular)/triangular_solve | solution.py:60
  844.6 1.4 convolution_subtract_fusion.1
  847.5 56.3 %all-reduce.34.cloned.1.call-done = f32[512,256]{0,1:T(8,128)} async-done(((f32[512,256]{0,1:T(8,128)}), f32[512,256]{0,1:T(8,128)}) %all-reduce.34.cloned.1.call-update) | async-done | bytes 524304 | tf_op jit(solution)/shard_map/psum | solution.py:34
  903.7 1.7 dynamic-slice_select_fusion
  905.5 1.1 fusion.3
  907.5 41.7 %all-reduce.36.cloned.1.call-done = f32[256,256]{0,1:T(8,128)} async-done(((f32[256,256]{0,1:T(8,128)}), f32[256,256]{0,1:T(8,128)}) %all-reduce.36.cloned.1.call-update) | async-done | bytes 262160 | tf_op jit(solution)/shard_map/psum | solution.py:34
  949.3 1.6 fusion
  (162 shorter events, 35.5 us)
Async XLA Ops:
  9.2 9.0 copy-start.5
  9.2 9.0 copy-start.6
  11.8 21.7 %all-to-all-start = ((bf16[8,64,440]{2,1,0:T(8,128)(2,1)}), bf16[8,64,440]{2,1,0:T(8,128)(2,1)S(1)}, u32[]{:S(2)}, u32[]{:S(2)}) async-start(bf16[8,64,440]{2,1,0:T(8,128)(2,1)} %bitcast.1), calls=%async_computation | async-start | bytes 1048576 | tf_op jit(solution)/shard_map/all_to_all | solution.py:82
  18.1 123.0 %all-reduce.14.cloned.1.call-start = ((), (), s32[]{:S(2)}) async-start(), calls=%async_computation.1 | async-start | bytes 524288 | tf_op jit(solution)/shard_map/psum | solution.py:34
  34.6 1.6 collective-permute-start
  36.4 14.0 %collective-permute-start.1 = (bf16[512,440]{1,0:T(8,128)(2,1)S(1)}, bf16[512,440]{1,0:T(8,128)(2,1)S(1)}, u32[]{:S(2)}, u32[]{:S(2)}) collective-permute-start(bf16[512,440]{1,0:T(8,128)(2,1)S(1)} %maximum_select_fusion.2), channel_id=1, source_target_pairs={{0,2},{1,3},{2,0},{3,1},{4,6},{5,7},{6,4},{7,5},{8,10},{9,11},{10,... | collective-permute-start | bytes 1351688 | tf_op jit(solution)/shard_map/ppermute | solution.py:21
  51.4 41.5 %collective-permute-start.2 = (bf16[1024,440]{0,1:T(8,128)(2,1)S(1)}, bf16[1024,440]{0,1:T(8,128)(2,1)S(1)}, u32[]{:S(2)}, u32[]{:S(2)}) collective-permute-start(bf16[1024,440]{0,1:T(8,128)(2,1)S(1)} %copy.66), channel_id=1, source_target_pairs={{0,4},{1,5},{2,6},{3,7},{4,0},{5,1},{6,2},{7,3},{8,12},{9,13},{10,... | collective-permute-start | bytes 2703368 | tf_op jit(solution)/shard_map/ppermute | solution.py:21
  99.2 163.2 %all-reduce.16.cloned.1.call-start = ((), (), s32[]{:S(2)}) async-start(), calls=%async_computation.2 | async-start | bytes 1048576 | tf_op jit(solution)/shard_map/psum | solution.py:34
  206.1 101.8 %all-reduce.18.cloned.1.call-start = ((), (), s32[]{:S(2)}) async-start(), calls=%async_computation.3 | async-start | bytes 524288 | tf_op jit(solution)/shard_map/psum | solution.py:34
  264.1 90.3 %all-reduce.20.cloned.1.call-start = ((), (), s32[]{:S(2)}) async-start(), calls=%async_computation.4 | async-start | bytes 524288 | tf_op jit(solution)/shard_map/psum | solution.py:34
  310.6 165.3 %all-reduce.22.cloned.1.call-start = ((), (), s32[]{:S(2)}) async-start(), calls=%async_computation.5 | async-start | bytes 1048576 | tf_op jit(solution)/shard_map/psum | solution.py:34
  419.5 101.9 %all-reduce.24.cloned.1.call-start = ((), (), s32[]{:S(2)}) async-start(), calls=%async_computation.6 | async-start | bytes 524288 | tf_op jit(solution)/shard_map/psum | solution.py:34
  477.6 90.3 %all-reduce.26.cloned.1.call-start = ((), (), s32[]{:S(2)}) async-start(), calls=%async_computation.7 | async-start | bytes 524288 | tf_op jit(solution)/shard_map/psum | solution.py:34
  524.0 165.4 %all-reduce.28.cloned.1.call-start = ((), (), s32[]{:S(2)}) async-start(), calls=%async_computation.8 | async-start | bytes 1048576 | tf_op jit(solution)/shard_map/psum | solution.py:34
  633.1 101.8 %all-reduce.30.cloned.1.call-start = ((), (), s32[]{:S(2)}) async-start(), calls=%async_computation.9 | async-start | bytes 524288 | tf_op jit(solution)/shard_map/psum | solution.py:34
  691.1 90.3 %all-reduce.32.cloned.1.call-start = ((), (), s32[]{:S(2)}) async-start(), calls=%async_computation.10 | async-start | bytes 524288 | tf_op jit(solution)/shard_map/psum | solution.py:34
  736.6 107.5 %copy-start.4 = (f32[256,512]{1,0:T(8,128)}, f32[256,512]{1,0:T(8,128)S(1)}, u32[]{:S(2)}) copy-start(f32[256,512]{1,0:T(8,128)S(1)} %get-tuple-element.120) | copy-start | bytes 1572868
  737.5 166.2 %all-reduce.34.cloned.1.call-start = ((), (), s32[]{:S(2)}) async-start(), calls=%async_computation.11 | async-start | bytes 1048576 | tf_op jit(solution)/shard_map/psum | solution.py:34
  844.6 60.9 %copy-start.1 = (f32[512,256]{0,1:T(8,128)S(1)}, f32[512,256]{0,1:T(8,128)}, u32[]{:S(2)}) copy-start(f32[512,256]{0,1:T(8,128)} %all-reduce.16.cloned.1.call-done) | copy-start | bytes 1572868
  844.6 60.9 %copy-start.2 = (f32[512,256]{0,1:T(8,128)S(1)}, f32[512,256]{0,1:T(8,128)}, u32[]{:S(2)}) copy-start(f32[512,256]{0,1:T(8,128)} %all-reduce.22.cloned.1.call-done) | copy-start | bytes 1572868
  844.6 60.9 %copy-start.3 = (f32[512,256]{0,1:T(8,128)S(1)}, f32[512,256]{0,1:T(8,128)}, u32[]{:S(2)}) copy-start(f32[512,256]{0,1:T(8,128)} %all-reduce.28.cloned.1.call-done) | copy-start | bytes 1572868
  847.4 101.9 %all-reduce.36.cloned.1.call-start = ((), (), s32[]{:S(2)}) async-start(), calls=%async_computation.12 | async-start | bytes 524288 | tf_op jit(solution)/shard_map/psum | solution.py:34
  903.7 45.5 %copy-start = (f32[512,256]{0,1:T(8,128)S(1)}, f32[512,256]{0,1:T(8,128)}, u32[]{:S(2)}) copy-start(f32[512,256]{0,1:T(8,128)} %all-reduce.34.cloned.1.call-done) | copy-start | bytes 1572868
Sparse Core Ops, SparseCore 0:
  99.3 41.8 all-reduce.13
  206.2 56.1 all-reduce.15
  265.9 41.8 all-reduce.17
  311.4 42.9 all-reduce.19
  419.7 56.1 all-reduce.21
  479.5 41.8 all-reduce.23
  524.9 42.9 all-reduce.25
  633.2 56.1 all-reduce.27
  692.9 41.8 all-reduce.29
  738.4 42.9 all-reduce.31
  847.5 56.1 all-reduce.33
  907.4 41.8 all-reduce.35
